TPU v7x, 128 devices: a whole 4x4x4 slice. The times are simulated.
128 devices in a mesh: seq: 4 (over x), ctx: 32 (over z, y, core).
Axes of the slice: x: 4, y: 4, z: 4, core: 2. Of those that a mesh axis runs over, the one named last changes fastest.
Arguments:
- delta_query: bfloat16 [4, 4096, 2048], P('seq', 'ctx'), may hold values from -6 to 6
- delta_key: bfloat16 [4, 4096, 2048], P('seq', 'ctx'), may hold values from -6 to 6
- delta_value: bfloat16 [4, 4096, 4096], P('seq', 'ctx'), may hold values from -6 to 6
- delta_gate: bfloat16 [4, 4096, 4096], P('seq', 'ctx'), may hold values from -6 to 6
- delta_beta: float32 [4, 32, 4096], P('seq', None, 'ctx'), may hold values from 0 to 1
- delta_decay: float32 [4, 32, 4096], P('seq', None, 'ctx'), may hold values from -2 to 0
- norm_gain: float32 [128], replicated, may hold values from 0.5 to 1.5
- attention_query: bfloat16 [4, 4096, 4096], P('seq', 'ctx'), may hold values from -4 to 4
- attention_key_value: bfloat16 [4, 4096, 1024], P('seq', 'ctx'), may hold values from -4 to 4
- attention_gate: bfloat16 [4, 4096, 4096], P('seq', 'ctx'), may hold values from -6 to 6
- moe_input: bfloat16 [4, 4096, 2048], P('seq', 'ctx'), may hold values from -6 to 6
- routes: int32 [4, 4096, 10], P('seq', 'ctx'), may hold values from 0 to 127, all different within a row; in each aligned block of 128 rows (0 to 127, 128 to 255, ..., all dimensions but the last counted through in order) at most 16 rows name the same one
- drop_mask: int32 [4, 4096, 10], P('seq', 'ctx'), may hold values 0 or 1
- route_weights: float32 [4, 4096, 10], P('seq', 'ctx'), may hold values from 0.05 to 0.5
- w_gate: bfloat16 [128, 2048, 512], P(('seq', 'ctx')), may hold values from -0.125 to 0.125
- w_up: bfloat16 [128, 2048, 512], P(('seq', 'ctx')), may hold values from -0.125 to 0.125
- w_down: bfloat16 [128, 512, 2048], P(('seq', 'ctx')), may hold values from -0.25 to 0.25
Outputs:
- delta_out: bfloat16 [4, 4096, 4096], P('seq', 'ctx')
- attn_out: bfloat16 [4, 4096, 4096], P('seq', 'ctx')
- moe_out: bfloat16 [4, 4096, 2048], P('seq', 'ctx')
Inputs may be any that keep to these rules, and one draw needn't show every extreme that they name: `routes`: within the rows of one device (aligned blocks of 128 positions), each token names 10 different experts and no expert is named more than 16 times; in some block some expert is named exactly 16 times. `drop_mask`: 1 keeps the chosen expert, 0 drops it.
All inputs are finite; a program needn't handle non-finite values. No bound on the sum of `drop_mask` on one device may be relied on, other than what follows from the above.
Results may differ from a plain program's by a relative error of at most 0.011.
Values may be sent and summed in bfloat16 or wider, within the bound.
No kernel may reach another device: no remote copies, remote signals or barrier semaphores. Data moves between devices by JAX's collectives and lax.ppermute only.
A program may use at most 384 MiB of HBM per device.

v0:
```python
import math

import jax
import jax.numpy as jnp
from jax import lax
from jax.sharding import PartitionSpec as P

HV = 32
HKD = 16
DK = 128
DV = 128
QUERY_HEADS = 16
KEY_VALUE_HEADS = 2
HEAD_WIDTH = 256
SPAN = 64


precise = lax.Precision.HIGHEST


def prefix(x, axis, combine, identity):
    length, index = (lax.axis_size(axis), lax.axis_index(axis))
    everything = jax.tree.map(lambda part: lax.all_gather(part, axis), x)
    start = jax.tree.map(
        lambda part, zero: jnp.broadcast_to(jnp.asarray(zero, part.dtype), part.shape), x, identity
    )

    def lap(k, before):
        reached = k < index
        new = combine(before, jax.tree.map(lambda part: part[k], everything))
        return jax.tree.map(lambda a, b: jnp.where(reached, a, b), new, before)

    return lax.fori_loop(0, length, lap, start)


def shifted(block, axis, distance):
    devices = range(lax.axis_size(axis))
    route = [(i - distance, i) for i in devices if i - distance in devices]
    return lax.ppermute(block, axis, route)


def unit_rows(matrix):
    return matrix / jnp.sqrt(jnp.sum(matrix * matrix, axis=-1, keepdims=True) + 1e-06)


def span_terms(query_rows, keys, value_rows, beta, decay):
    size = decay.shape[-1]
    key_dim = keys.shape[-1]
    value_dim = value_rows.shape[-1]
    cumulative = jnp.cumsum(decay, axis=-1)
    place_list = jnp.arange(size)
    lower = place_list[:, None] >= place_list[None, :]
    strict = place_list[:, None] > place_list[None, :]
    spread = cumulative[..., :, None] - cumulative[..., None, :]
    decay_ratio = jnp.exp(jnp.where(lower, spread, -1e30))
    key_key = jnp.einsum("...ik,...jk->...ij", keys, keys, precision=precise)
    query_key = jnp.einsum("...ik,...jk->...ij", query_rows, keys, precision=precise)
    system = jnp.eye(size, dtype=jnp.float32) + jnp.where(
        strict, beta[..., :, None] * decay_ratio * key_key, 0.0
    )
    retained = jnp.exp(cumulative)
    right_side = jnp.concatenate(
        [beta[..., None] * value_rows, (beta * retained)[..., None] * keys], axis=-1
    )
    solved = jax.scipy.linalg.solve_triangular(system, right_side, lower=True, unit_diagonal=True)
    new_values = solved[..., :value_dim]
    new_keys = solved[..., value_dim:]
    mixing = decay_ratio * query_key
    query_eff = retained[..., None] * query_rows - jnp.einsum(
        "...ij,...jk->...ik", mixing, new_keys, precision=precise
    )
    direct = jnp.einsum("...ij,...jv->...iv", mixing, new_values, precision=precise)
    tail_keys = jnp.exp(cumulative[..., -1:] - cumulative)[..., None] * keys
    carry_a = retained[..., -1:, None] * jnp.eye(key_dim, dtype=jnp.float32) - jnp.einsum(
        "...ck,...cl->...kl", new_keys, tail_keys, precision=precise
    )
    carry_b = jnp.einsum("...cv,...cl->...vl", new_values, tail_keys, precision=precise)
    return (query_eff, direct, carry_a, carry_b)


def compose(earlier, later):
    joined_a = jnp.einsum("hij,hjk->hik", earlier[0], later[0], precision=precise)
    joined_b = jnp.einsum("hvk,hkl->hvl", earlier[1], later[0], precision=precise) + later[1]
    return (joined_a, joined_b)


def gated_norm(outputs, delta_gate, norm_gain):
    scale = lax.rsqrt(jnp.mean(outputs * outputs, axis=-1, keepdims=True) + 1e-06)
    gate_vals = delta_gate.astype(jnp.float32).reshape(outputs.shape)
    normed = outputs * scale * norm_gain * jax.nn.silu(gate_vals)
    return normed.astype(jnp.bfloat16).reshape(delta_gate.shape)


def delta_mixer(
    delta_query, delta_key, delta_value, delta_gate, delta_beta, delta_decay, norm_gain
):
    token_count = delta_query.shape[1]
    n_spans = token_count // SPAN
    head_repeat = HV // HKD
    query_rows = unit_rows(delta_query[0].astype(jnp.float32).reshape(token_count, HKD, DK)) * (
        1.0 / math.sqrt(DK)
    )
    query_rows = jnp.repeat(query_rows, head_repeat, axis=1)
    keys = jnp.repeat(
        unit_rows(delta_key[0].astype(jnp.float32).reshape(token_count, HKD, DK)),
        head_repeat,
        axis=1,
    )
    value_rows = delta_value[0].astype(jnp.float32).reshape(token_count, HV, DV)

    def to_spans(array):
        return array.reshape(n_spans, SPAN, HV, array.shape[-1]).transpose(2, 0, 1, 3)

    query_eff, direct, carry_a, carry_b = span_terms(
        to_spans(query_rows),
        to_spans(keys),
        to_spans(value_rows),
        delta_beta[0].reshape(HV, n_spans, SPAN),
        delta_decay[0].reshape(HV, n_spans, SPAN),
    )
    identity = jnp.broadcast_to(jnp.eye(DK, dtype=jnp.float32), (HV, DK, DK))
    zero_state = jnp.zeros((HV, DV, DK), jnp.float32)
    starts_a = [identity]
    starts_b = [zero_state]
    for span_id in range(n_spans):
        starts_a.append(
            jnp.einsum("hij,hjk->hik", starts_a[-1], carry_a[:, span_id], precision=precise)
        )
        starts_b.append(
            jnp.einsum("hvk,hkl->hvl", starts_b[-1], carry_a[:, span_id], precision=precise)
            + carry_b[:, span_id]
        )
    incoming = prefix((starts_a[-1], starts_b[-1]), "ctx", compose, (identity, zero_state))
    state_in = incoming[1]
    before_a = jnp.stack(starts_a[:-1], axis=1)
    before_b = jnp.stack(starts_b[:-1], axis=1)
    states = jnp.einsum("hvk,hckl->hcvl", state_in, before_a, precision=precise) + before_b
    outputs = jnp.einsum("hcik,hcvk->hciv", query_eff, states, precision=precise) + direct
    outputs = outputs.transpose(1, 2, 0, 3).reshape(token_count, HV, DV)
    return gated_norm(outputs, delta_gate, norm_gain)


def window_attention(attention_query, window_key_value, attention_gate, base):
    local_sequences = attention_query.shape[0]
    token_count = attention_query.shape[1]
    head_groups = QUERY_HEADS // KEY_VALUE_HEADS
    query_rows = attention_query.reshape(
        local_sequences, token_count, KEY_VALUE_HEADS, head_groups, HEAD_WIDTH
    )
    key_value = window_key_value.reshape(
        local_sequences, 2 * token_count, 2, KEY_VALUE_HEADS, HEAD_WIDTH
    )
    scores = jnp.einsum(
        "stkgd,sukd->skgtu", query_rows, key_value[:, :, 0], preferred_element_type=jnp.float32
    ) * (1.0 / math.sqrt(HEAD_WIDTH))
    query_pos = base + jnp.arange(token_count, dtype=jnp.int32)
    key_pos = base - token_count + jnp.arange(2 * token_count, dtype=jnp.int32)
    visible = (
        (key_pos[None, :] <= query_pos[:, None])
        & (key_pos[None, :] > query_pos[:, None] - token_count)
        & (key_pos[None, :] >= 0)
    )
    scores = jnp.where(visible, scores, -jnp.inf)
    row_max = jnp.max(scores, axis=-1, keepdims=True)
    lifted = jnp.exp(scores - row_max)
    probs = (lifted / jnp.sum(lifted, axis=-1, keepdims=True)).astype(jnp.bfloat16)
    mixed = jnp.einsum(
        "skgtu,sukd->stkgd", probs, key_value[:, :, 1], preferred_element_type=jnp.float32
    )
    gated = mixed * jax.nn.sigmoid(attention_gate.astype(jnp.float32).reshape(mixed.shape))
    return gated.astype(jnp.bfloat16).reshape(attention_query.shape)


def slot_numbers(expert_ids, experts):
    row_count = expert_ids.shape[0]
    onehot = (expert_ids[:, None] == jnp.arange(experts, dtype=jnp.int32)[None, :]).astype(
        jnp.bfloat16
    )
    place_list = jnp.arange(row_count, dtype=jnp.int32)
    before = (place_list[:, None] > place_list[None, :]).astype(jnp.bfloat16)
    earlier = jnp.dot(before, onehot, preferred_element_type=jnp.float32)
    return jnp.sum(earlier * onehot.astype(jnp.float32), axis=1).astype(jnp.int32)


def expert_layer(moe_input, routes, drop_mask, route_weights, w_gate, w_up, w_down):
    token_count = moe_input.shape[1]
    width = moe_input.shape[2]
    top_count = routes.shape[2]
    n_seq = lax.axis_size("seq")
    n_ctx = lax.axis_size("ctx")
    n_dev = n_seq * n_ctx
    capacity = max(2, token_count * top_count * 8 // (n_dev * 5))
    expert_ids = routes[0].reshape(-1)
    keep_flags = drop_mask[0].reshape(-1)
    target = expert_ids * capacity + slot_numbers(expert_ids, n_dev)
    rows = jnp.repeat(moe_input[0], top_count, axis=0) * keep_flags[:, None].astype(jnp.bfloat16)
    outgoing = jnp.zeros((n_dev * capacity, width), jnp.bfloat16).at[target].set(rows)
    arrived = lax.all_to_all(
        outgoing.reshape(n_dev, capacity, width),
        ("seq", "ctx"),
        split_axis=0,
        concat_axis=0,
        tiled=True,
    )
    flat_rows = arrived.reshape(-1, width)
    gate_part = jnp.dot(flat_rows, w_gate[0], preferred_element_type=jnp.float32)
    up_part = jnp.dot(flat_rows, w_up[0], preferred_element_type=jnp.float32)
    hidden = (jax.nn.silu(gate_part) * up_part).astype(jnp.bfloat16)
    result = jnp.dot(hidden, w_down[0], preferred_element_type=jnp.float32).astype(jnp.bfloat16)
    returned = lax.all_to_all(
        result.reshape(arrived.shape), ("seq", "ctx"), split_axis=0, concat_axis=0, tiled=True
    )
    results = returned.reshape(n_dev * capacity, width)[target]
    weights = keep_flags.astype(jnp.float32) * route_weights[0].reshape(-1)
    combined = jnp.einsum(
        "tkd,tk->td",
        results.reshape(token_count, top_count, width).astype(jnp.float32),
        weights.reshape(token_count, top_count),
    )
    return combined.astype(jnp.bfloat16)[None]


def body(
    delta_query,
    delta_key,
    delta_value,
    delta_gate,
    delta_beta,
    delta_decay,
    norm_gain,
    attention_query,
    attention_key_value,
    attention_gate,
    moe_input,
    routes,
    drop_mask,
    route_weights,
    w_gate,
    w_up,
    w_down,
):
    delta_out = delta_mixer(
        delta_query, delta_key, delta_value, delta_gate, delta_beta, delta_decay, norm_gain
    )
    previous = shifted(attention_key_value, "ctx", 1)
    window_key_value = jnp.concatenate([previous, attention_key_value], axis=1)
    base = lax.axis_index("ctx") * attention_query.shape[1]
    attn_out = window_attention(attention_query, window_key_value, attention_gate, base)
    moe_out = expert_layer(moe_input, routes, drop_mask, route_weights, w_gate, w_up, w_down)
    return (delta_out, attn_out, moe_out)


def solution(mesh):
    placed = (
        P("seq", "ctx", None),
        P("seq", "ctx", None),
        P("seq", "ctx", None),
        P("seq", "ctx", None),
        P("seq", None, "ctx"),
        P("seq", None, "ctx"),
        P(),
        P("seq", "ctx", None),
        P("seq", "ctx", None),
        P("seq", "ctx", None),
        P("seq", "ctx", None),
        P("seq", "ctx", None),
        P("seq", "ctx", None),
        P("seq", "ctx", None),
        P(("seq", "ctx"), None, None),
        P(("seq", "ctx"), None, None),
        P(("seq", "ctx"), None, None),
    )
    return jax.shard_map(
        body,
        mesh=mesh,
        in_specs=placed,
        out_specs=(P("seq", "ctx", None), P("seq", "ctx", None), P("seq", "ctx", None)),
        check_vma=False,
    )
```

profile of v0, /device:TPU:14, one launch (start us, length us, event | category | flops | bytes accessed | tf_op | source)
XLA Modules:
  0.0 1325.0 jit_solution(12630235698171251444)
XLA Ops:
  38.8 10.3 add_bitcast_fusion
  49.1 134.3 %custom-call.4 = f32[32,2,1,64,64]{0,3,4,2,1:T(8,128)} custom-call(f32[32,2,1,64,64]{0,4,3,2,1:T(8,128)} %get-tuple-element.150), custom_call_target="InvertDiagBlocksLowerTriangular" | custom-call | tf_op jit(solution)/shard_map/jit(_solve_triangular)/vmap(vmap())/triangular_solve | solution.py:65
  195.5 20.5 %multiply_subtract_fusion = f32[32,2,128,128]{3,2,1,0:T(8,128)S(1)} fusion(f32[128,128]{1,0:T(8,128)S(1)} %fusion.77, f32[32,2]{1,0:T(8,128)S(1)} %bitcast.185, f32[32,2,64,256]{3,2,1,0:T(8,128)S(1)} %fusion.16, f32[32,2,64,128]{3,2,1,0:T(8,128)S(1)} %bitcast.162, f32[32,2,64]{2,1,0:T(2,128)S(1)} %copy.93), kind=kOutput, calls=%fused_computation.31 | convolution fusion | flops 807927808 | bytes 8503296 | tf_op jit(solution)/shard_map/...ck,...cl->...kl/dot_general | solution.py:74
  222.9 9.4 fusion.53
  246.0 9.9 reshape.287
  256.0 19.9 %scatter_custom_fusion = bf16[2048,2048]{1,0:T(8,128)(2,1)} fusion(s32[1280]{0:T(1024)S(1)} %fusion.80, bf16[1280,2048]{1,0:T(8,128)(2,1)} %reshape.287, bf16[]{:T(256)} %constant.73.clone.1, bf16[1280]{0:T(1024)(128)(2,1)S(1)} %convert_element_type.125), kind=kCustom, calls=%fused_computation.16 | custom fusion | flops 2621440 | bytes 13635586 | tf_op jit(solution)/shard_map/scatter | solution.py:197
  275.9 125.6 %all_to_all.10 = bf16[128,16,2048]{2,1,0:T(8,128)(2,1)S(1)} all-to-all(bf16[128,16,2048]{2,1,0:T(8,128)(2,1)} %bitcast.163), channel_id=1, replica_groups=mesh['seq'=4,'ctx'=32] {'seq','ctx'}, dimensions={0} | all-to-all | bytes 16777216 | tf_op jit(solution)/shard_map/all_to_all | solution.py:198
  418.0 11.5 all-to-all-start.1
  453.3 102.1 %collective-permute-done = bf16[1,128,1024]{1,2,0:T(8,128)(2,1)} collective-permute-done((bf16[1,128,1024]{1,2,0:T(8,128)(2,1)S(1)}, bf16[1,128,1024]{1,2,0:T(8,128)(2,1)}, u32[]{:S(2)}, u32[]{:S(2)}) %collective-permute-start) | collective-permute-done | bytes 262176 | tf_op jit(solution)/shard_map/ppermute | solution.py:39
  560.0 16.0 %gather_fusion = bf16[1280,2048]{1,0:T(8,128)(2,1)} fusion(bf16[2048,2048]{1,0:T(8,128)(2,1)} %bitcast.44, s32[2048]{0:T(1024)S(1)} %copy-done.33), kind=kCustom, calls=%fused_computation | custom fusion | bytes 10490880 | tf_op jit(solution)/shard_map/gather | solution.py:213
  576.0 9.6 reshape.292
  591.5 18.1 %all-gather.5.cloned.1.call-done = f32[1024,128,128]{2,1,0:T(8,128)} async-done(((f32[32,128,128]{2,1,0:T(8,128)}), f32[1024,128,128]{2,1,0:T(8,128)}) %all-gather.5.cloned.1.call-update) | async-done | bytes 67108880 | tf_op jit(solution)/shard_map/all_gather | solution.py:23
  609.6 208.9 %all-gather.7.cloned.1.call-done = f32[1024,128,128]{2,1,0:T(8,128)} async-done(((f32[32,128,128]{2,1,0:T(8,128)}), f32[1024,128,128]{2,1,0:T(8,128)}) %all-gather.7.cloned.1.call-update) | async-done | bytes 67108880 | tf_op jit(solution)/shard_map/all_gather | solution.py:23
  818.5 468.3 %while.14 = (s32[]{:T(128)}, f32[32,128,128]{1,2,0:T(8,128)}, s32[]{:T(128)}, f32[32,32,128,128]{3,2,1,0:T(8,128)}, f32[32,32,128,128]{3,2,1,0:T(8,128)}, /*index=5*/s32[]{:T(128)}, s32[]{:T(128)}) while((s32[]{:T(128)}, f32[32,128,128]{1,2,0:T(8,128)}, s32[]{:T(128)}, f32[32,32,128,128]{3,2,1,0:T(8,128)}, ...), condition=%wide.region_4.5_spmd.clone, body=%wide.region_3.4_spmd.clone.sunk | while | flops 807403520 | bytes 23070828 | solution.py:33
  826.1 7.0 fusion.108
  884.6 7.0 fusion.108
  899.3 7.0 fusion.108
  913.9 7.0 fusion.108
  928.5 7.0 fusion.108
  943.1 7.0 fusion.108
  957.8 7.0 fusion.108
  972.4 7.0 fusion.108
  987.0 7.0 fusion.108
  1074.8 7.0 fusion.108
  1089.4 7.0 fusion.108
  1104.0 7.0 fusion.108
  1118.7 7.0 fusion.108
  1162.5 7.0 fusion.108
  1177.2 7.0 fusion.108
  1191.8 7.0 fusion.108
  1206.4 7.0 fusion.108
  1295.1 9.4 multiply_reduce_fusion
  (290 shorter events, 484.9 us)
Async XLA Ops:
  7.2 404.0 %copy-start = (bf16[1,512,2048]{2,1,0:T(8,128)(2,1)S(1)}, bf16[1,512,2048]{2,1,0:T(8,128)(2,1)}, u32[]{:S(2)}) copy-start(bf16[1,512,2048]{2,1,0:T(8,128)(2,1)} %param.35) | copy-start | bytes 6291460
  7.2 602.5 %all-gather.5.cloned.1.call-start = ((), (), s32[]{:S(2)}) async-start(), calls=%async_computation.2 | async-start | bytes 69206016 | tf_op jit(solution)/shard_map/all_gather | solution.py:23
  17.1 4.8 copy-start.2
  17.1 4.8 copy-start.29
  27.7 2.3 copy-start.3
  34.8 4.0 copy-start.28
  34.8 4.0 copy-start.30
  34.8 4.0 copy-start.31
  34.9 4.0 copy-start.32
  183.4 5.4 copy-start.19
  189.4 2.2 copy-start.15
  191.6 3.9 copy-start.4
  195.5 20.5 %copy-start.6 = (f32[32,2,64,256]{3,2,1,0:T(8,128)}, f32[32,2,64,256]{3,2,1,0:T(8,128)S(1)}, u32[]{:S(2)}) copy-start(f32[32,2,64,256]{3,2,1,0:T(8,128)S(1)} %fusion.16) | copy-start | bytes 12582916
  222.8 595.7 %all-gather.7.cloned.1.call-start = ((), (), s32[]{:S(2)}) async-start(), calls=%async_computation.3 | async-start | bytes 69206016 | tf_op jit(solution)/shard_map/all_gather | solution.py:23
  222.9 9.4 copy-start.9
  275.8 125.6 %copy-start.38 = (bf16[1,2048,512]{2,1,0:T(8,128)(2,1)S(1)}, bf16[1,2048,512]{2,1,0:T(8,128)(2,1)}, u32[]{:S(2)}) copy-start(bf16[1,2048,512]{2,1,0:T(8,128)(2,1)} %param.33) | copy-start | bytes 6291460
  401.5 4.5 copy-start.39
  418.0 11.5 copy-start.26
  418.0 142.0 %all-to-all-start.1 = ((bf16[128,16,2048]{2,1,0:T(8,128)(2,1)}), bf16[128,16,2048]{2,1,0:T(8,128)(2,1)}, u32[]{:S(2)}, u32[]{:S(2)}) async-start(bf16[128,16,2048]{2,1,0:T(8,128)(2,1)} %bitcast.170), calls=%async_computation.1 | async-start | bytes 16777216 | tf_op jit(solution)/shard_map/all_to_all | solution.py:210
  429.7 125.7 %collective-permute-start = (bf16[1,128,1024]{1,2,0:T(8,128)(2,1)S(1)}, bf16[1,128,1024]{1,2,0:T(8,128)(2,1)}, u32[]{:S(2)}, u32[]{:S(2)}) collective-permute-start(bf16[1,128,1024]{1,2,0:T(8,128)(2,1)S(1)} %copy.104), channel_id=1, source_target_pairs={{0,1},{1,2},{2,3},{3,4},{4,5},{5,6},{6,7},{7,8},{8,9},{9,10},{10,1... | collective-permute-start | bytes 786440 | tf_op jit(solution)/shard_map/ppermute | solution.py:39
  431.7 5.5 copy-start.36
  431.7 6.1 copy-start.37
  437.8 5.3 copy-start.7
  443.2 3.7 copy-start.20
  446.8 2.6 copy-start.21
  450.7 105.7 %copy-start.22 = (bf16[16,8,16,256]{3,2,1,0:T(8,128)(2,1)S(1)}, bf16[16,8,16,256]{3,2,1,0:T(8,128)(2,1)}, u32[]{:S(2)}) copy-start(bf16[16,8,16,256]{3,2,1,0:T(8,128)(2,1)} %copy.134) | copy-start | bytes 3145732
  1288.4 6.7 copy-start.11
  1288.4 6.7 copy-start.16
  1288.4 6.7 copy-start.17
  1288.4 6.7 copy-start.27
  1311.0 2.9 copy-start.23
  1311.0 6.8 copy-start.1
  (12 other events, 15.9 us)
Sparse Core Ops, SparseCore 0:
  223.0 386.6 all-gather.4
  611.9 206.5 all-gather.6
where the time goes:
time: 1340 us; the launch traced here: 1330 us
  local copies, waits for them, and re-layouts  331 us (25%)
  waiting for transfers between devices  329 us (25%)
  matrix products  328 us (24%)
  other arithmetic  183 us (14%)
  blocking collectives  126 us (9%)
  between operations  15.1 us (1%)
  starting transfers between devices  13.6 us (1%)
    all_gather x2, waiting for transfers between devices, prefix(): everything = jax.tree.map(lambda part: lax.all_gather(part, axis), x)  227 us
    dot_general x32, matrix products, compose(): jnp.einsum('hvk,hkl->hvl', earlier[1], later[0], precision=precise)  225 us
    dynamic_slice x64, local copies, waits for them, and re-layouts, lap(): new = combine(before, jax.tree.map(lambda part: part[k], everything))  193 us
    another operation x4, other arithmetic, span_terms(): jax.scipy.linalg.solve_triangular(system, right_side, lower=True, unit_di...  145 us
    all_to_all x1, blocking collectives, expert_layer(): lax.all_to_all(outgoing.reshape(n_dev, capacity, width), ('seq', 'ctx'),...  126 us
    ppermute x1, waiting for transfers between devices, shifted(): return lax.ppermute(block, axis, route)  102 us
    while x32, local copies, waits for them, and re-layouts  50.9 us
  transfers between devices with their start and end apart: 4, of which 3 were waited for; matrix products, arithmetic and copies ran while one was open for 9% of the time, Pallas kernels for 0%

commit v1 on v0

--- a/solution.py
+++ b/solution.py
@@ -18,19 +18,23 @@
 precise = lax.Precision.HIGHEST
 
 
-def prefix(x, axis, combine, identity):
+def carried_state(a, b, axis):
     length, index = (lax.axis_size(axis), lax.axis_index(axis))
-    everything = jax.tree.map(lambda part: lax.all_gather(part, axis), x)
-    start = jax.tree.map(
-        lambda part, zero: jnp.broadcast_to(jnp.asarray(zero, part.dtype), part.shape), x, identity
-    )
-
-    def lap(k, before):
-        reached = k < index
-        new = combine(before, jax.tree.map(lambda part: part[k], everything))
-        return jax.tree.map(lambda a, b: jnp.where(reached, a, b), new, before)
-
-    return lax.fori_loop(0, length, lap, start)
+    distance = 1
+    while distance < length:
+        route = [(i, i + distance) for i in range(length - distance)]
+        reached = index >= distance
+        if 2 * distance >= length:
+            b_before = lax.ppermute(b, axis, route)
+            b = jnp.einsum("hvk,hkl->hvl", b_before, a, precision=precise) + b
+        else:
+            a_before, b_before = lax.ppermute((a, b), axis, route)
+            joined_a = jnp.einsum("hij,hjk->hik", a_before, a, precision=precise)
+            joined_b = jnp.einsum("hvk,hkl->hvl", b_before, a, precision=precise) + b
+            a = jnp.where(reached, joined_a, a)
+            b = jnp.where(reached, joined_b, b)
+        distance *= 2
+    return lax.ppermute(b, axis, [(i, i + 1) for i in range(length - 1)])
 
 
 def shifted(block, axis, distance):
@@ -78,12 +82,6 @@
     return (query_eff, direct, carry_a, carry_b)
 
 
-def compose(earlier, later):
-    joined_a = jnp.einsum("hij,hjk->hik", earlier[0], later[0], precision=precise)
-    joined_b = jnp.einsum("hvk,hkl->hvl", earlier[1], later[0], precision=precise) + later[1]
-    return (joined_a, joined_b)
-
-
 def gated_norm(outputs, delta_gate, norm_gain):
     scale = lax.rsqrt(jnp.mean(outputs * outputs, axis=-1, keepdims=True) + 1e-06)
     gate_vals = delta_gate.astype(jnp.float32).reshape(outputs.shape)
@@ -130,8 +128,7 @@
             jnp.einsum("hvk,hkl->hvl", starts_b[-1], carry_a[:, span_id], precision=precise)
             + carry_b[:, span_id]
         )
-    incoming = prefix((starts_a[-1], starts_b[-1]), "ctx", compose, (identity, zero_state))
-    state_in = incoming[1]
+    state_in = carried_state(starts_a[-1], starts_b[-1], "ctx")
     before_a = jnp.stack(starts_a[:-1], axis=1)
     before_b = jnp.stack(starts_b[:-1], axis=1)
     states = jnp.einsum("hvk,hckl->hcvl", state_in, before_a, precision=precise) + before_b

time: 1340 us -> 846 us (0.63)
  local copies, waits for them, and re-layouts: 331 us -> 84.1 us
  matrix products: 328 us -> 149 us
  blocking collectives: 126 us -> 0 us
  starting transfers between devices: 13.6 us -> 117 us
  waiting for transfers between devices: 329 us -> 297 us
  between operations: 15.1 us -> 1.69 us
    ppermute x0 -> x10, waiting for transfers between devices: none -> 297 us  [the longest x8 184 us: carried_state(): a_before, b_before = lax.ppermute((a, b), axis, route)]
    all_gather x2 -> x0, waiting for transfers between devices: 227 us -> none  [prefix(): everything = jax.tree.map(lambda part: lax.all_gather(part, axis), x)]
    dynamic_slice x64 -> x0, local copies, waits for them, and re-layouts: 193 us -> none  [lap(): new = combine(before, jax.tree.map(lambda part: part[k], everything))]
    dot_general x32 -> x9, matrix products: 225 us -> 52.4 us  [the longest x4 25.1 us: carried_state(): joined_b = jnp.einsum('hvk,hkl->hvl', b_before, a, precision=precise) + b]
    all_to_all x1 -> x0, blocking collectives: 126 us -> none  [expert_layer(): lax.all_to_all(outgoing.reshape(n_dev, capacity, width), ('seq', 'ctx'),...]
    ppermute x1, waiting for transfers between devices: 102 us -> 0.01 us  [shifted(): return lax.ppermute(block, axis, route)]
    while x32 -> x0, local copies, waits for them, and re-layouts: 50.9 us -> none
    all_to_all x1, starting transfers between devices: 11.5 us -> 60.1 us  [expert_layer(): lax.all_to_all(result.reshape(arrived.shape), ('seq', 'ctx'), split_axis=...]
  transfers between devices with their start and end apart: 4 -> 13, of which waited for: 3 -> 7; matrix products, arithmetic and copies ran while one was open for 9% -> 41% of each run, Pallas kernels for 0% -> 0%
where the time goes in v1:
time: 846 us; the launch traced here: 832 us
  waiting for transfers between devices  297 us (35%)
  other arithmetic  183 us (22%)
  matrix products  149 us (18%)
  starting transfers between devices  117 us (14%)
  local copies, waits for them, and re-layouts  84.1 us (10%)
    ppermute x8, waiting for transfers between devices, carried_state(): a_before, b_before = lax.ppermute((a, b), axis, route)  184 us
    another operation x4, other arithmetic, span_terms(): jax.scipy.linalg.solve_triangular(system, right_side, lower=True, unit_di...  145 us
    ppermute x1, waiting for transfers between devices, carried_state(): return lax.ppermute(b, axis, [(i, i + 1) for i in range(length - 1)])  72 us
    all_to_all x1, starting transfers between devices, expert_layer(): lax.all_to_all(result.reshape(arrived.shape), ('seq', 'ctx'), split_axis=...  60.1 us
    ppermute x1, waiting for transfers between devices, carried_state(): b_before = lax.ppermute(b, axis, route)  41.2 us
    ppermute x8, starting transfers between devices, carried_state(): a_before, b_before = lax.ppermute((a, b), axis, route)  36.1 us
    dot_general x4, matrix products, carried_state(): joined_b = jnp.einsum('hvk,hkl->hvl', b_before, a, precision=precise) + b  25.1 us
    dot_general x4, matrix products, carried_state(): joined_a = jnp.einsum('hij,hjk->hik', a_before, a, precision=precise)  21.4 us
  transfers between devices with their start and end apart: 13, of which 7 were waited for; matrix products, arithmetic and copies ran while one was open for 41% of the time, Pallas kernels for 0%

profile of v1, /device:TPU:14, one launch (start us, length us, event | category | flops | bytes accessed | tf_op | source)
XLA Modules:
  0.0 832.4 jit_solution(12377715017096277436)
XLA Ops:
  9.2 9.8 %reshape.287 = bf16[1280,2048]{1,0:T(8,128)(2,1)} reshape(bf16[128,10,2048]{2,1,0:T(8,128)(2,1)} %broadcast_in_dim.82) | data formatting | bytes 10485760 | tf_op jit(solution)/shard_map/reshape | solution.py:193
  19.0 19.6 %scatter_custom_fusion = bf16[2048,2048]{1,0:T(8,128)(2,1)} fusion(s32[1280]{0:T(1024)S(1)} %fusion.73, bf16[1280,2048]{1,0:T(8,128)(2,1)} %reshape.287, bf16[]{:T(256)} %constant.58.clone.1, bf16[1280]{0:T(1024)(128)(2,1)S(1)} %convert_element_type.125), kind=kCustom, calls=%fused_computation.5 | custom fusion | flops 2621440 | bytes 13635586 | tf_op jit(solution)/shard_map/scatter | solution.py:194
  38.7 11.2 %all-to-all-start = ((bf16[128,16,2048]{2,1,0:T(8,128)(2,1)}), bf16[128,16,2048]{2,1,0:T(8,128)(2,1)}, u32[]{:S(2)}, u32[]{:S(2)}) async-start(bf16[128,16,2048]{2,1,0:T(8,128)(2,1)} %bitcast.160), calls=%async_computation | async-start | bytes 16777216 | tf_op jit(solution)/shard_map/all_to_all | solution.py:195
  79.1 10.2 %add_bitcast_fusion = (f32[32,2,1,64,64]{0,4,3,2,1:T(8,128)}, f32[32,2,64,64]{0,3,2,1:T(8,128)}) fusion(f32[32,2,64,64]{0,3,2,1:T(8,128)} %copy.79, f32[64,64]{1,0:T(8,128)S(1)} %copy-done.28, f32[32,2,64]{0,2,1:T(8,128)S(1)} %copy.78, f32[64,64]{1,0:T(8,128)S(1)} %get-tuple-element.24, f32[32,2,64]{0,2,1:T(8,128)S(1)} %copy.74, ...), kind=kLoop, calls=%fused_computation.21 | loop fusion | flops 2359296 | bytes 4272128 | tf_op jit(solution)/shard_map/jit(_solve_triangular)/vmap(vmap())/triangular_solve | solution.py:69
  89.3 134.0 %custom-call.4 = f32[32,2,1,64,64]{0,3,4,2,1:T(8,128)} custom-call(f32[32,2,1,64,64]{0,4,3,2,1:T(8,128)} %get-tuple-element.12), custom_call_target="InvertDiagBlocksLowerTriangular" | custom-call | tf_op jit(solution)/shard_map/jit(_solve_triangular)/vmap(vmap())/triangular_solve | solution.py:69
  235.8 7.6 fusion.42
  243.4 8.0 multiply_subtract_fusion
  268.0 16.7 %collective-permute-done = f32[32,128,128]{2,1,0:T(8,128)} collective-permute-done((f32[32,128,128]{2,1,0:T(8,128)}, f32[32,128,128]{2,1,0:T(8,128)}, u32[]{:S(2)}, u32[]{:S(2)}) %collective-permute-start) | collective-permute-done | bytes 2097184 | tf_op jit(solution)/shard_map/ppermute | solution.py:31
  284.7 6.4 add_select_fusion.3
  294.6 22.9 %collective-permute-done.2 = f32[32,128,128]{2,1,0:T(8,128)} collective-permute-done((f32[32,128,128]{2,1,0:T(8,128)}, f32[32,128,128]{2,1,0:T(8,128)}, u32[]{:S(2)}, u32[]{:S(2)}) %collective-permute-start.2) | collective-permute-done | bytes 2097184 | tf_op jit(solution)/shard_map/ppermute | solution.py:31
  317.5 6.3 convolution_select_fusion.2
  327.6 14.3 %collective-permute-done.1 = f32[32,128,128]{2,1,0:T(8,128)} collective-permute-done((f32[32,128,128]{2,1,0:T(8,128)}, f32[32,128,128]{2,1,0:T(8,128)}, u32[]{:S(2)}, u32[]{:S(2)}) %collective-permute-start.1) | collective-permute-done | bytes 2097184 | tf_op jit(solution)/shard_map/ppermute | solution.py:31
  341.9 6.4 add_select_fusion.2
  348.3 6.5 collective-permute-start.3
  354.8 32.0 %collective-permute-done.4 = f32[32,128,128]{2,1,0:T(8,128)} collective-permute-done((f32[32,128,128]{2,1,0:T(8,128)}, f32[32,128,128]{2,1,0:T(8,128)}, u32[]{:S(2)}, u32[]{:S(2)}) %collective-permute-start.4) | collective-permute-done | bytes 2097184 | tf_op jit(solution)/shard_map/ppermute | solution.py:31
  386.8 6.3 convolution_select_fusion.1
  393.2 8.2 collective-permute-start.6
  401.4 6.4 add_select_fusion.1
  411.6 7.7 fusion.28
  419.3 8.8 %multiply_convert_fusion = bf16[2048,512]{1,0:T(8,128)(2,1)S(1)} fusion(f32[2048,512]{1,0:T(8,128)S(1)} %fusion.28, bf16[2048,2048]{1,0:T(8,128)(2,1)} %bitcast.37, bf16[1,2048,512]{2,1,0:T(8,128)(2,1)S(1)} %copy-done.42), kind=kOutput, calls=%fused_computation.18 | convolution fusion | flops 4301258752 | bytes 16777216 | tf_op jit(solution)/shard_map/dot_general | solution.py:204
  428.2 6.8 convolution_convert_fusion
  434.9 60.1 %all-to-all-start.1 = ((bf16[128,16,2048]{2,1,0:T(8,128)(2,1)}), bf16[128,16,2048]{2,1,0:T(8,128)(2,1)}, u32[]{:S(2)}, u32[]{:S(2)}) async-start(bf16[128,16,2048]{2,1,0:T(8,128)(2,1)} %bitcast.167), calls=%async_computation.1 | async-start | bytes 16777216 | tf_op jit(solution)/shard_map/all_to_all | solution.py:207
  507.3 5.8 add_select_fusion
  524.6 5.9 fusion.40
  532.3 98.3 %collective-permute-done.8 = f32[32,128,128]{2,1,0:T(8,128)} collective-permute-done((f32[32,128,128]{2,1,0:T(8,128)S(1)}, f32[32,128,128]{2,1,0:T(8,128)}, u32[]{:S(2)}, u32[]{:S(2)}) %collective-permute-start.8) | collective-permute-done | bytes 2097184 | tf_op jit(solution)/shard_map/ppermute | solution.py:31
  634.5 41.2 %collective-permute-done.7 = f32[32,128,128]{2,1,0:T(8,128)} collective-permute-done((f32[32,128,128]{2,1,0:T(8,128)}, f32[32,128,128]{2,1,0:T(8,128)}, u32[]{:S(2)}, u32[]{:S(2)}) %collective-permute-start.7) | collective-permute-done | bytes 2097184 | tf_op jit(solution)/shard_map/ppermute | solution.py:28
  675.7 5.8 fusion.50
  698.3 72.0 %collective-permute-done.9 = f32[32,128,128]{2,1,0:T(8,128)} collective-permute-done((f32[32,128,128]{2,1,0:T(8,128)}, f32[32,128,128]{2,1,0:T(8,128)}, u32[]{:S(2)}, u32[]{:S(2)}) %collective-permute-start.9) | collective-permute-done | bytes 2097184 | tf_op jit(solution)/shard_map/ppermute | solution.py:37
  770.6 6.8 bitcast_add_fusion
  777.5 9.5 %multiply_reduce_fusion = (f32[2,64,32]{1,0,2:T(2,128)S(1)}, f32[2,64,32,128]{3,1,0,2:T(8,128)}) fusion(f32[32,2,64,128]{3,2,1,0:T(8,128)S(1)} %copy-done.15, f32[32,2,128,128]{3,2,0,1:T(8,128)S(1)} %bitcast_add_fusion, f32[32,2,64,128]{3,2,1,0:T(8,128)S(1)} %copy-done.16, f32[32,2,64,128]{3,2,1,0:T(8,128)S(1)} %bitcast.162, f32[32,2,64]{2,1,0:T(2,128)S(1)} %copy-done.29), kind=kOutput, calls=%fused_computation.55 | convolution fusion | flops 807923712 | bytes 12615680 | tf_op jit(solution)/shard_map/hcik,hcvk->hciv/dot_general | solution.py:135
  801.2 15.3 %gather_fusion = bf16[1280,2048]{1,0:T(8,128)(2,1)} fusion(bf16[2048,2048]{1,0:T(8,128)(2,1)} %bitcast.42, s32[2048]{0:T(1024)S(1)} %copy-done.32), kind=kCustom, calls=%fused_computation | custom fusion | bytes 10490880 | tf_op jit(solution)/shard_map/gather | solution.py:210
  816.5 9.6 %reshape.292 = bf16[128,10,2048]{2,1,0:T(8,128)(2,1)} reshape(bf16[1280,2048]{1,0:T(8,128)(2,1)} %gather_fusion) | data formatting | bytes 10485760 | tf_op jit(solution)/shard_map/reshape | solution.py:214
  (190 shorter events, 144.0 us)
Async XLA Ops:
  0.6 427.5 %copy-start = (bf16[1,512,2048]{2,1,0:T(8,128)(2,1)S(1)}, bf16[1,512,2048]{2,1,0:T(8,128)(2,1)}, u32[]{:S(2)}) copy-start(bf16[1,512,2048]{2,1,0:T(8,128)(2,1)} %param.33) | copy-start | bytes 6291460
  19.0 19.6 %copy-start.35 = (s32[1280]{0:T(1024)}, s32[1280]{0:T(1024)S(1)}, u32[]{:S(2)}) copy-start(s32[1280]{0:T(1024)S(1)} %fusion.73) | copy-start | bytes 15364
  38.6 12.5 %copy-start.38 = (f32[1,32,128]{2,1,0:T(8,128)S(1)}, f32[1,32,128]{2,1,0:T(8,128)}, u32[]{:S(2)}) copy-start(f32[1,32,128]{2,1,0:T(8,128)} %param.22) | copy-start | bytes 49156
  38.6 14.0 %copy-start.39 = (f32[1,32,128]{2,1,0:T(8,128)S(1)}, f32[1,32,128]{2,1,0:T(8,128)}, u32[]{:S(2)}) copy-start(f32[1,32,128]{2,1,0:T(8,128)} %param.21) | copy-start | bytes 49156
  38.6 15.3 %copy-start.25 = (bf16[1,128,2048]{2,1,0:T(8,128)(2,1)S(1)}, bf16[1,128,2048]{2,1,0:T(8,128)(2,1)}, u32[]{:S(2)}) copy-start(bf16[1,128,2048]{2,1,0:T(8,128)(2,1)} %param.17) | copy-start | bytes 1572868
  38.7 373.0 %all-to-all-start = ((bf16[128,16,2048]{2,1,0:T(8,128)(2,1)}), bf16[128,16,2048]{2,1,0:T(8,128)(2,1)}, u32[]{:S(2)}, u32[]{:S(2)}) async-start(bf16[128,16,2048]{2,1,0:T(8,128)(2,1)} %bitcast.160), calls=%async_computation | async-start | bytes 16777216 | tf_op jit(solution)/shard_map/all_to_all | solution.py:195
  223.3 5.8 copy-start.19
  235.8 7.6 copy-start.5
  257.1 27.7 %collective-permute-start = (f32[32,128,128]{2,1,0:T(8,128)}, f32[32,128,128]{2,1,0:T(8,128)}, u32[]{:S(2)}, u32[]{:S(2)}) collective-permute-start(f32[32,128,128]{2,1,0:T(8,128)} %fusion.23), channel_id=1, source_target_pairs={{0,1},{1,2},{2,3},{3,4},{4,5},{5,6},{6,7},{7,8},{8,9},{9,10},{10,1... | collective-permute-start | bytes 6291464 | tf_op jit(solution)/shard_map/ppermute | solution.py:31
  264.6 52.9 %collective-permute-start.2 = (f32[32,128,128]{2,1,0:T(8,128)}, f32[32,128,128]{2,1,0:T(8,128)}, u32[]{:S(2)}, u32[]{:S(2)}) collective-permute-start(f32[32,128,128]{2,1,0:T(8,128)} %fusion.38), channel_id=1, source_target_pairs={{0,1},{1,2},{2,3},{3,4},{4,5},{5,6},{6,7},{7,8},{8,9},{9,10},{10,1... | collective-permute-start | bytes 6291464 | tf_op jit(solution)/shard_map/ppermute | solution.py:31
  291.2 50.7 %collective-permute-start.1 = (f32[32,128,128]{2,1,0:T(8,128)}, f32[32,128,128]{2,1,0:T(8,128)}, u32[]{:S(2)}, u32[]{:S(2)}) collective-permute-start(f32[32,128,128]{2,1,0:T(8,128)} %add_select_fusion.3), channel_id=1, source_target_pairs={{0,2},{1,3},{2,4},{3,5},{4,6},{5,7},{6,8},{7,9},{8,10},{9,11},{10,... | collective-permute-start | bytes 6291464 | tf_op jit(solution)/shard_map/ppermute | solution.py:31
  323.8 63.0 %collective-permute-start.4 = (f32[32,128,128]{2,1,0:T(8,128)}, f32[32,128,128]{2,1,0:T(8,128)}, u32[]{:S(2)}, u32[]{:S(2)}) collective-permute-start(f32[32,128,128]{2,1,0:T(8,128)} %convolution_select_fusion.2), channel_id=1, source_target_pairs={{0,2},{1,3},{2,4},{3,5},{4,6},{5,7},{6,8},{7,9},{8,10},{9,11},{10,... | collective-permute-start | bytes 6291464 | tf_op jit(solution)/shard_map/ppermute | solution.py:31
  348.3 53.1 %collective-permute-start.3 = (f32[32,128,128]{2,1,0:T(8,128)}, f32[32,128,128]{2,1,0:T(8,128)}, u32[]{:S(2)}, u32[]{:S(2)}) collective-permute-start(f32[32,128,128]{2,1,0:T(8,128)} %add_select_fusion.2), channel_id=1, source_target_pairs={{0,4},{1,5},{2,6},{3,7},{4,8},{5,9},{6,10},{7,11},{8,12},{9,13},{1... | collective-permute-start | bytes 6291464 | tf_op jit(solution)/shard_map/ppermute | solution.py:31
  393.2 104.1 %collective-permute-start.6 = (f32[32,128,128]{2,1,0:T(8,128)}, f32[32,128,128]{2,1,0:T(8,128)}, u32[]{:S(2)}, u32[]{:S(2)}) collective-permute-start(f32[32,128,128]{2,1,0:T(8,128)} %convolution_select_fusion.1), channel_id=1, source_target_pairs={{0,4},{1,5},{2,6},{3,7},{4,8},{5,9},{6,10},{7,11},{8,12},{9,13},{1... | collective-permute-start | bytes 6291464 | tf_op jit(solution)/shard_map/ppermute | solution.py:31
  407.8 99.4 %collective-permute-start.5 = (f32[32,128,128]{2,1,0:T(8,128)}, f32[32,128,128]{2,1,0:T(8,128)}, u32[]{:S(2)}, u32[]{:S(2)}) collective-permute-start(f32[32,128,128]{2,1,0:T(8,128)} %add_select_fusion.1), channel_id=1, source_target_pairs={{0,8},{1,9},{2,10},{3,11},{4,12},{5,13},{6,14},{7,15},{8,16},{9,17... | collective-permute-start | bytes 6291464 | tf_op jit(solution)/shard_map/ppermute | solution.py:31
  411.6 7.7 copy-start.42
  434.9 60.1 %copy-start.27 = (bf16[1,128,1024]{2,1,0:T(8,128)(2,1)S(1)}, bf16[1,128,1024]{2,1,0:T(8,128)(2,1)}, u32[]{:S(2)}) copy-start(bf16[1,128,1024]{2,1,0:T(8,128)(2,1)} %param.25) | copy-start | bytes 786436
  434.9 366.3 %all-to-all-start.1 = ((bf16[128,16,2048]{2,1,0:T(8,128)(2,1)}), bf16[128,16,2048]{2,1,0:T(8,128)(2,1)}, u32[]{:S(2)}, u32[]{:S(2)}) async-start(bf16[128,16,2048]{2,1,0:T(8,128)(2,1)} %bitcast.167), calls=%async_computation.1 | async-start | bytes 16777216 | tf_op jit(solution)/shard_map/all_to_all | solution.py:207
  495.2 198.3 %collective-permute-start.10 = (bf16[1,128,1024]{1,2,0:T(8,128)(2,1)S(1)}, bf16[1,128,1024]{1,2,0:T(8,128)(2,1)}, u32[]{:S(2)}, u32[]{:S(2)}) collective-permute-start(bf16[1,128,1024]{1,2,0:T(8,128)(2,1)S(1)} %copy.94), channel_id=1, source_target_pairs={{0,1},{1,2},{2,3},{3,4},{4,5},{5,6},{6,7},{7,8},{8,9},{9,10},{10,1... | collective-permute-start | bytes 786440 | tf_op jit(solution)/shard_map/ppermute | solution.py:43
  502.3 128.4 %collective-permute-start.8 = (f32[32,128,128]{2,1,0:T(8,128)S(1)}, f32[32,128,128]{2,1,0:T(8,128)}, u32[]{:S(2)}, u32[]{:S(2)}) collective-permute-start(f32[32,128,128]{2,1,0:T(8,128)S(1)} %convolution_select_fusion), channel_id=1, source_target_pairs={{0,8},{1,9},{2,10},{3,11},{4,12},{5,13},{6,14},{7,15},{8,16},{9,17... | collective-permute-start | bytes 6291464 | tf_op jit(solution)/shard_map/ppermute | solution.py:31
  513.1 162.6 %collective-permute-start.7 = (f32[32,128,128]{2,1,0:T(8,128)}, f32[32,128,128]{2,1,0:T(8,128)}, u32[]{:S(2)}, u32[]{:S(2)}) collective-permute-start(f32[32,128,128]{2,1,0:T(8,128)} %add_select_fusion), channel_id=1, source_target_pairs={{0,16},{1,17},{2,18},{3,19},{4,20},{5,21},{6,22},{7,23},{8,24},{9,... | collective-permute-start | bytes 6291464 | tf_op jit(solution)/shard_map/ppermute | solution.py:28
  524.6 5.9 copy-start.20
  634.5 49.6 %copy-start.41 = (f32[128]{0:T(128)S(1)}, f32[128]{0:T(128)}, u32[]{:S(2)}) copy-start(f32[128]{0:T(128)} %param.23) | copy-start | bytes 1540
  634.5 49.6 %copy-start.6 = (f32[32,2,64,256]{3,2,1,0:T(8,128)S(1)}, f32[32,2,64,256]{3,2,1,0:T(8,128)}, u32[]{:S(2)}) copy-start(f32[32,2,64,256]{3,2,1,0:T(8,128)} %copy-done.5) | copy-start | bytes 12582916
  634.5 49.6 %copy-start.7 = (f32[32,2,64,64]{3,2,1,0:T(8,128)S(1)}, f32[32,2,64,64]{3,2,1,0:T(8,128)}, u32[]{:S(2)}) copy-start(f32[32,2,64,64]{3,2,1,0:T(8,128)} %copy.84) | copy-start | bytes 3145732
  681.5 88.8 %collective-permute-start.9 = (f32[32,128,128]{2,1,0:T(8,128)}, f32[32,128,128]{2,1,0:T(8,128)}, u32[]{:S(2)}, u32[]{:S(2)}) collective-permute-start(f32[32,128,128]{2,1,0:T(8,128)} %fusion.50), channel_id=1, source_target_pairs={{0,1},{1,2},{2,3},{3,4},{4,5},{5,6},{6,7},{7,8},{8,9},{9,10},{10,1... | collective-permute-start | bytes 6291464 | tf_op jit(solution)/shard_map/ppermute | solution.py:37
  698.3 72.3 %copy-start.11 = (f32[32,128,128]{2,1,0:T(8,128)S(1)}, f32[32,128,128]{2,1,0:T(8,128)}, u32[]{:S(2)}) copy-start(f32[32,128,128]{2,1,0:T(8,128)} %copy-done.10) | copy-start | bytes 6291460
  770.6 6.8 copy-start.9
  770.6 6.8 copy-start.15
  770.6 6.8 copy-start.16
  770.6 6.8 copy-start.29
  826.1 6.0 copy-start.1
  (24 other events, 80.5 us)

commit v2 on v0

--- a/solution.py
+++ b/solution.py
@@ -12,25 +12,10 @@
 QUERY_HEADS = 16
 KEY_VALUE_HEADS = 2
 HEAD_WIDTH = 256
-SPAN = 64
+SPAN = 32
 
 
 precise = lax.Precision.HIGHEST
-
-
-def prefix(x, axis, combine, identity):
-    length, index = (lax.axis_size(axis), lax.axis_index(axis))
-    everything = jax.tree.map(lambda part: lax.all_gather(part, axis), x)
-    start = jax.tree.map(
-        lambda part, zero: jnp.broadcast_to(jnp.asarray(zero, part.dtype), part.shape), x, identity
-    )
-
-    def lap(k, before):
-        reached = k < index
-        new = combine(before, jax.tree.map(lambda part: part[k], everything))
-        return jax.tree.map(lambda a, b: jnp.where(reached, a, b), new, before)
-
-    return lax.fori_loop(0, length, lap, start)
 
 
 def shifted(block, axis, distance):
@@ -78,12 +63,6 @@
     return (query_eff, direct, carry_a, carry_b)
 
 
-def compose(earlier, later):
-    joined_a = jnp.einsum("hij,hjk->hik", earlier[0], later[0], precision=precise)
-    joined_b = jnp.einsum("hvk,hkl->hvl", earlier[1], later[0], precision=precise) + later[1]
-    return (joined_a, joined_b)
-
-
 def gated_norm(outputs, delta_gate, norm_gain):
     scale = lax.rsqrt(jnp.mean(outputs * outputs, axis=-1, keepdims=True) + 1e-06)
     gate_vals = delta_gate.astype(jnp.float32).reshape(outputs.shape)
@@ -91,52 +70,54 @@
     return normed.astype(jnp.bfloat16).reshape(delta_gate.shape)
 
 
+def span_prefix(a, b):
+    count = a.shape[1]
+    eye = jnp.broadcast_to(jnp.eye(a.shape[-1], dtype=a.dtype), a.shape)
+    distance = 1
+    while distance < count:
+        a_before = jnp.concatenate([eye[:, :distance], a[:, : count - distance]], axis=1)
+        b_before = jnp.concatenate([jnp.zeros_like(b[:, :distance]), b[:, : count - distance]], axis=1)
+        b = jnp.einsum("hcvk,hckl->hcvl", b_before, a, precision=precise) + b
+        if 2 * distance < count:
+            a = jnp.einsum("hcij,hcjk->hcik", a_before, a, precision=precise)
+        distance *= 2
+    return jnp.concatenate([jnp.zeros_like(b[:, :1]), b[:, : count - 1]], axis=1)
+
+
 def delta_mixer(
     delta_query, delta_key, delta_value, delta_gate, delta_beta, delta_decay, norm_gain
 ):
     token_count = delta_query.shape[1]
-    n_spans = token_count // SPAN
     head_repeat = HV // HKD
-    query_rows = unit_rows(delta_query[0].astype(jnp.float32).reshape(token_count, HKD, DK)) * (
-        1.0 / math.sqrt(DK)
-    )
-    query_rows = jnp.repeat(query_rows, head_repeat, axis=1)
-    keys = jnp.repeat(
-        unit_rows(delta_key[0].astype(jnp.float32).reshape(token_count, HKD, DK)),
-        head_repeat,
-        axis=1,
-    )
-    value_rows = delta_value[0].astype(jnp.float32).reshape(token_count, HV, DV)
+    heads_here = HV // lax.axis_size("ctx")
+    query_raw = jnp.repeat(delta_query[0].reshape(token_count, HKD, DK), head_repeat, axis=1)
+    key_raw = jnp.repeat(delta_key[0].reshape(token_count, HKD, DK), head_repeat, axis=1)
+    value_raw = delta_value[0].reshape(token_count, HV, DV)
+    joined = jnp.concatenate([query_raw, key_raw, value_raw], axis=-1)
+    joined = lax.all_to_all(joined, "ctx", split_axis=1, concat_axis=0, tiled=True)
+    rates = jnp.stack([delta_beta[0], delta_decay[0]], axis=0)
+    rates = lax.all_to_all(rates, "ctx", split_axis=1, concat_axis=2, tiled=True)
+    length = joined.shape[0]
+    n_spans = length // SPAN
+    joined = joined.astype(jnp.float32)
+    query_rows = unit_rows(joined[..., :DK]) * (1.0 / math.sqrt(DK))
+    keys = unit_rows(joined[..., DK : 2 * DK])
+    value_rows = joined[..., 2 * DK :]
 
     def to_spans(array):
-        return array.reshape(n_spans, SPAN, HV, array.shape[-1]).transpose(2, 0, 1, 3)
+        return array.reshape(n_spans, SPAN, heads_here, array.shape[-1]).transpose(2, 0, 1, 3)
 
     query_eff, direct, carry_a, carry_b = span_terms(
         to_spans(query_rows),
         to_spans(keys),
         to_spans(value_rows),
-        delta_beta[0].reshape(HV, n_spans, SPAN),
-        delta_decay[0].reshape(HV, n_spans, SPAN),
-    )
-    identity = jnp.broadcast_to(jnp.eye(DK, dtype=jnp.float32), (HV, DK, DK))
-    zero_state = jnp.zeros((HV, DV, DK), jnp.float32)
-    starts_a = [identity]
-    starts_b = [zero_state]
-    for span_id in range(n_spans):
-        starts_a.append(
-            jnp.einsum("hij,hjk->hik", starts_a[-1], carry_a[:, span_id], precision=precise)
-        )
-        starts_b.append(
-            jnp.einsum("hvk,hkl->hvl", starts_b[-1], carry_a[:, span_id], precision=precise)
-            + carry_b[:, span_id]
-        )
-    incoming = prefix((starts_a[-1], starts_b[-1]), "ctx", compose, (identity, zero_state))
-    state_in = incoming[1]
-    before_a = jnp.stack(starts_a[:-1], axis=1)
-    before_b = jnp.stack(starts_b[:-1], axis=1)
-    states = jnp.einsum("hvk,hckl->hcvl", state_in, before_a, precision=precise) + before_b
+        rates[0].reshape(heads_here, n_spans, SPAN),
+        rates[1].reshape(heads_here, n_spans, SPAN),
+    )
+    states = span_prefix(carry_a, carry_b)
     outputs = jnp.einsum("hcik,hcvk->hciv", query_eff, states, precision=precise) + direct
-    outputs = outputs.transpose(1, 2, 0, 3).reshape(token_count, HV, DV)
+    outputs = outputs.transpose(1, 2, 0, 3).reshape(length, heads_here, DV)
+    outputs = lax.all_to_all(outputs, "ctx", split_axis=0, concat_axis=1, tiled=True)
     return gated_norm(outputs, delta_gate, norm_gain)
 
 

time: 1340 us -> 668 us (0.50)
  waiting for transfers between devices: 329 us -> 106 us
  local copies, waits for them, and re-layouts: 331 us -> 171 us
  blocking collectives: 126 us -> 0 us
  other arithmetic: 183 us -> 71.8 us
  matrix products: 328 us -> 266 us
  starting transfers between devices: 13.6 us -> 41.3 us
    all_gather x2 -> x0, waiting for transfers between devices: 227 us -> none  [prefix(): everything = jax.tree.map(lambda part: lax.all_gather(part, axis), x)]
    dynamic_slice x64 -> x0, local copies, waits for them, and re-layouts: 193 us -> none  [lap(): new = combine(before, jax.tree.map(lambda part: part[k], everything))]
    all_to_all x1 -> x0, blocking collectives: 126 us -> none  [expert_layer(): lax.all_to_all(outgoing.reshape(n_dev, capacity, width), ('seq', 'ctx'),...]
    another operation x4 -> x3, other arithmetic: 145 us -> 22.2 us  [span_terms(): jax.scipy.linalg.solve_triangular(system, right_side, lower=True, unit_di...]
    slice x2 -> x20, local copies, waits for them, and re-layouts: 0.23 us -> 83.5 us  [the longest x6 41.1 us: span_prefix(): a[:, :count - distance]]
    dot_general x37 -> x13, matrix products: 242 us -> 170 us  [the longest x7 98 us: span_prefix(): b = jnp.einsum('hcvk,hckl->hcvl', b_before, a, precision=precise) + b]
    while x32 -> x0, local copies, waits for them, and re-layouts: 50.9 us -> none
    all_to_all x0 -> x4, starting transfers between devices: none -> 31.7 us  [the longest x1 8.55 us: delta_mixer(): lax.all_to_all(rates, 'ctx', split_axis=1, concat_axis=2, tiled=True)]
  transfers between devices with their start and end apart: 4 -> 6, of which waited for: 3 -> 3; matrix products, arithmetic and copies ran while one was open for 9% -> 72% of each run, Pallas kernels for 0% -> 0%
where the time goes in v2:
time: 668 us; the launch traced here: 658 us
  matrix products  266 us (40%)
  local copies, waits for them, and re-layouts  171 us (26%)
  waiting for transfers between devices  106 us (16%)
  other arithmetic  71.8 us (11%)
  starting transfers between devices  41.3 us (6%)
    ppermute x1, waiting for transfers between devices, shifted(): return lax.ppermute(block, axis, route)  99.4 us
    dot_general x7, matrix products, span_prefix(): b = jnp.einsum('hcvk,hckl->hcvl', b_before, a, precision=precise) + b  98 us
    dot_general x6, matrix products, span_prefix(): a = jnp.einsum('hcij,hcjk->hcik', a_before, a, precision=precise)  72 us
    slice x6, local copies, waits for them, and re-layouts, span_prefix(): a[:, :count - distance]  41.1 us
    slice x7, local copies, waits for them, and re-layouts, span_prefix(): b[:, :count - distance]  38.1 us
    another operation x3, other arithmetic, span_terms(): jax.scipy.linalg.solve_triangular(system, right_side, lower=True, unit_di...  22.2 us
    scatter x1, other arithmetic, expert_layer(): jnp.zeros((n_dev * capacity, width), jnp.bfloat16).at[target].set(rows)  19.8 us
    dot_general x1, matrix products, delta_mixer(): jnp.einsum('hcik,hcvk->hciv', query_eff, states, precision=precise) + direct  15.8 us
  transfers between devices with their start and end apart: 6, of which 3 were waited for; matrix products, arithmetic and copies ran while one was open for 72% of the time, Pallas kernels for 0%

profile of v2, /device:TPU:14, one launch (start us, length us, event | category | flops | bytes accessed | tf_op | source)
XLA Modules:
  0.0 658.4 jit_solution(17046235421530866659)
XLA Ops:
  2.2 8.5 %all-to-all-start = ((f32[2,32,128]{2,0,1:T(2,128)}), f32[2,32,128]{2,0,1:T(2,128)S(1)}, u32[]{:S(2)}, u32[]{:S(2)}) async-start(f32[2,32,128]{2,0,1:T(2,128)} %copy.114), calls=%async_computation | async-start | bytes 65536 | tf_op jit(solution)/shard_map/all_to_all | solution.py:99
  25.4 7.6 %all-to-all-start.1 = ((bf16[128,32,384]{2,0,1:T(8,128)(2,1)}), bf16[128,32,384]{2,0,1:T(8,128)(2,1)}, u32[]{:S(2)}, u32[]{:S(2)}) async-start(bf16[128,32,384]{2,0,1:T(8,128)(2,1)} %copy.120), calls=%async_computation.1 | async-start | bytes 6291456 | tf_op jit(solution)/shard_map/all_to_all | solution.py:97
  38.9 9.8 %reshape.560 = bf16[1280,2048]{1,0:T(8,128)(2,1)} reshape(bf16[128,10,2048]{2,1,0:T(8,128)(2,1)} %broadcast_in_dim.46) | data formatting | bytes 10485760 | tf_op jit(solution)/shard_map/reshape | solution.py:177
  49.0 19.8 %scatter_custom_fusion = bf16[2048,2048]{1,0:T(8,128)(2,1)} fusion(s32[1280]{0:T(1024)S(1)} %fusion.112, bf16[1280,2048]{1,0:T(8,128)(2,1)} %reshape.560, bf16[]{:T(256)} %constant.29.clone.1, bf16[1280]{0:T(1024)(128)(2,1)S(1)} %convert_element_type.131), kind=kCustom, calls=%fused_computation.56 | custom fusion | flops 2621440 | bytes 13635586 | tf_op jit(solution)/shard_map/scatter | solution.py:178
  103.7 22.1 %custom-call.4 = f32[128,1,32,32]{0,2,3,1:T(8,128)S(1)} custom-call(f32[128,1,32,32]{0,3,2,1:T(8,128)} %get-tuple-element.26), custom_call_target="InvertDiagBlocksLowerTriangular" | custom-call | tf_op jit(solution)/shard_map/jit(_solve_triangular)/vmap()/triangular_solve | solution.py:50
  137.2 14.1 %fusion.92 = f32[128,128,128]{2,1,0:T(8,128)S(1)} fusion(f32[1,128,32,256]{3,2,1,0:T(8,128)S(1)} %fusion.76, f32[128,32,128]{2,1,0:T(8,128)S(1)} %bitcast.219, f32[128,32]{1,0:T(8,128)S(1)} %copy.128), kind=kOutput, calls=%fused_computation.107 | convolution fusion | flops 805830656 | bytes 12648448 | tf_op jit(solution)/shard_map/...cv,...cl->...vl/dot_general | solution.py:62
  151.3 14.2 %fusion.89 = f32[128,128,128]{2,1,0:T(8,128)S(1)} fusion(f32[1,128,32,256]{3,2,1,0:T(8,128)S(1)} %fusion.76, f32[128,32,128]{2,1,0:T(8,128)S(1)} %bitcast.220, f32[128,32]{1,0:T(8,128)S(1)} %copy.128), kind=kOutput, calls=%fused_computation.104 | convolution fusion | flops 805830656 | bytes 12648448 | tf_op jit(solution)/shard_map/...ck,...cl->...kl/dot_general | solution.py:59
  173.9 14.1 %fusion.54 = f32[128,128,128]{2,1,0:T(8,128)} fusion(f32[128,128,128]{2,1,0:T(8,128)} %copy-done.8, f32[128,128,128]{2,1,0:T(8,128)S(1)} %fusion.89, f32[128,128]{1,0:T(8,128)S(1)} %fusion.108, f32[128]{0:T(128)S(1)} %get-tuple-element.30, f32[1,127,128,128]{3,2,1,0:T(8,128)} %slice.140), kind=kOutput, calls=%fused_computation.68 | convolution fusion | flops 3227516928 | bytes 33554944 | tf_op jit(solution)/shard_map/hcvk,hckl->hcvl/dot_general | solution.py:80
  187.9 7.8 %slice.143 = f32[1,127,128,128]{3,2,1,0:T(8,128)} slice(f32[1,128,128,128]{3,2,1,0:T(8,128)} %fusion.43), slice={[0:1], [0:127], [0:128], [0:128]} | slice | bytes 16646144 | tf_op jit(solution)/shard_map/slice | solution.py:78
  199.9 12.6 %fusion = f32[128,128,128]{2,1,0:T(8,128)} fusion(f32[1,127,128,128]{3,2,1,0:T(8,128)} %slice.143, f32[1,1,128,128]{3,2,1,0:T(8,128)S(1)} %fusion.109, f32[128,128,128]{2,1,0:T(8,128)S(1)} %fusion.89, f32[128,128]{1,0:T(8,128)S(1)} %fusion.108, f32[128]{0:T(128)S(1)} %get-tuple-element.30), kind=kOutput, calls=%fused_computation.3 | convolution fusion | flops 3227516928 | bytes 25231872 | tf_op jit(solution)/shard_map/hcij,hcjk->hcik/dot_general | solution.py:82
  212.5 16.7 %fusion.57 = f32[128,128,128]{2,1,0:T(8,128)} fusion(f32[128,128,128]{2,1,0:T(8,128)} %fusion.54, f32[128,128,128]{2,1,0:T(8,128)} %fusion, f32[1,126,128,128]{3,2,1,0:T(8,128)} %slice.142), kind=kOutput, calls=%fused_computation.69 | convolution fusion | flops 3223322624 | bytes 33423360 | tf_op jit(solution)/shard_map/hcvk,hckl->hcvl/dot_general | solution.py:80
  239.7 12.0 %fusion.3 = f32[128,128,128]{2,1,0:T(8,128)} fusion(f32[128,128,128]{2,1,0:T(8,128)S(1)} %copy-done.1, f32[1,126,128,128]{3,2,1,0:T(8,128)} %slice.145, f32[1,2,128,128]{3,2,1,0:T(8,128)S(1)} %slice.113), kind=kOutput, calls=%fused_computation.7 | convolution fusion | flops 3223322624 | bytes 25165824 | tf_op jit(solution)/shard_map/hcij,hcjk->hcik/dot_general | solution.py:82
  251.8 7.7 %slice.147 = f32[1,124,128,128]{3,2,1,0:T(8,128)} slice(f32[1,128,128,128]{3,2,1,0:T(8,128)} %bitcast.212), slice={[0:1], [0:124], [0:128], [0:128]} | slice | bytes 16252928 | tf_op jit(solution)/shard_map/slice | solution.py:78
  259.4 14.0 %fusion.60 = f32[128,128,128]{2,1,0:T(8,128)} fusion(f32[128,128,128]{2,1,0:T(8,128)} %fusion.57, f32[128,128,128]{2,1,0:T(8,128)S(1)} %copy-done.2, f32[1,124,128,128]{3,2,1,0:T(8,128)} %slice.144), kind=kOutput, calls=%fused_computation.70 | convolution fusion | flops 3223322624 | bytes 33292288 | tf_op jit(solution)/shard_map/hcvk,hckl->hcvl/dot_general | solution.py:80
  273.5 7.3 %slice.146 = f32[1,120,128,128]{3,2,1,0:T(8,128)} slice(f32[1,128,128,128]{3,2,1,0:T(8,128)} %bitcast.224), slice={[0:1], [0:120], [0:128], [0:128]} | slice | bytes 15728640 | tf_op jit(solution)/shard_map/slice | solution.py:79
  280.8 12.1 %fusion.6 = f32[128,128,128]{2,1,0:T(8,128)} fusion(f32[128,128,128]{2,1,0:T(8,128)S(1)} %copy-done.2, f32[1,124,128,128]{3,2,1,0:T(8,128)} %slice.147, f32[1,4,128,128]{3,2,1,0:T(8,128)S(1)} %slice.116), kind=kOutput, calls=%fused_computation.11 | convolution fusion | flops 3223322624 | bytes 25165824 | tf_op jit(solution)/shard_map/hcij,hcjk->hcik/dot_general | solution.py:82
  292.9 7.4 %slice.149 = f32[1,120,128,128]{3,2,1,0:T(8,128)} slice(f32[1,128,128,128]{3,2,1,0:T(8,128)} %bitcast.213), slice={[0:1], [0:120], [0:128], [0:128]} | slice | bytes 15728640 | tf_op jit(solution)/shard_map/slice | solution.py:78
  300.3 13.6 %fusion.63 = f32[128,128,128]{2,1,0:T(8,128)} fusion(f32[128,128,128]{2,1,0:T(8,128)} %fusion.60, f32[128,128,128]{2,1,0:T(8,128)S(1)} %copy-done.3, f32[1,120,128,128]{3,2,1,0:T(8,128)} %slice.146), kind=kOutput, calls=%fused_computation.71 | convolution fusion | flops 3223322624 | bytes 33030144 | tf_op jit(solution)/shard_map/hcvk,hckl->hcvl/dot_general | solution.py:80
  321.2 11.1 %fusion.9 = f32[128,128,128]{2,1,0:T(8,128)} fusion(f32[128,128,128]{2,1,0:T(8,128)S(1)} %copy-done.3, f32[1,120,128,128]{3,2,1,0:T(8,128)S(1)} %copy-done.13, f32[1,8,128,128]{3,2,1,0:T(8,128)S(1)} %slice.119), kind=kOutput, calls=%fused_computation.15 | convolution fusion | flops 3223322624 | bytes 25165824 | tf_op jit(solution)/shard_map/hcij,hcjk->hcik/dot_general | solution.py:82
  339.4 13.4 %fusion.66 = f32[128,128,128]{2,1,0:T(8,128)} fusion(f32[128,128,128]{2,1,0:T(8,128)} %fusion.63, f32[128,128,128]{2,1,0:T(8,128)S(1)} %copy-done.4, f32[1,112,128,128]{3,2,1,0:T(8,128)} %slice.148), kind=kOutput, calls=%fused_computation.72 | convolution fusion | flops 3223322624 | bytes 32505856 | tf_op jit(solution)/shard_map/hcvk,hckl->hcvl/dot_general | solution.py:80
  359.3 12.2 %fusion.12 = f32[128,128,128]{2,1,0:T(8,128)} fusion(f32[128,128,128]{2,1,0:T(8,128)S(1)} %copy-done.4, f32[1,112,128,128]{3,2,1,0:T(8,128)} %slice.151, f32[1,16,128,128]{3,2,1,0:T(8,128)S(1)} %slice.122), kind=kOutput, calls=%fused_computation.19 | convolution fusion | flops 3223322624 | bytes 25165824 | tf_op jit(solution)/shard_map/hcij,hcjk->hcik/dot_general | solution.py:82
  377.9 13.1 %fusion.69 = f32[128,128,128]{2,1,0:T(8,128)} fusion(f32[128,128,128]{2,1,0:T(8,128)} %fusion.66, f32[128,128,128]{2,1,0:T(8,128)S(1)} %copy-done.5, f32[1,96,128,128]{3,2,1,0:T(8,128)} %slice.150), kind=kOutput, calls=%fused_computation.73 | convolution fusion | flops 3223322624 | bytes 31457280 | tf_op jit(solution)/shard_map/hcvk,hckl->hcvl/dot_general | solution.py:80
  396.0 12.0 %fusion.15 = f32[128,128,128]{2,1,0:T(8,128)} fusion(f32[128,128,128]{2,1,0:T(8,128)S(1)} %copy-done.5, f32[1,96,128,128]{3,2,1,0:T(8,128)} %slice.153, f32[1,32,128,128]{3,2,1,0:T(8,128)S(1)} %slice.125), kind=kOutput, calls=%fused_computation.23 | convolution fusion | flops 3223322624 | bytes 25165824 | tf_op jit(solution)/shard_map/hcij,hcjk->hcik/dot_general | solution.py:82
  407.9 13.0 %add_bitcast_fusion = f32[1,128,128,128]{3,2,1,0:T(8,128)S(1)} fusion(f32[128,128,128]{2,1,0:T(8,128)} %fusion.69, f32[128,128,128]{2,1,0:T(8,128)} %fusion.15, f32[1,64,128,128]{3,2,1,0:T(8,128)} %slice.152), kind=kOutput, calls=%fused_computation.43 | convolution fusion | flops 3223322624 | bytes 29360128 | tf_op jit(solution)/shard_map/hcvk,hckl->hcvl/dot_general | solution.py:80
  432.2 15.8 %fusion.18 = f32[128,32,128]{2,1,0:T(8,128)S(1)} fusion(f32[1,127,128,128]{3,2,1,0:T(8,128)} %slice.154, f32[128,32,128]{2,1,0:T(8,128)S(1)} %fusion.90, f32[128,32,128]{2,1,0:T(8,128)S(1)} %bitcast.232, f32[128,32]{1,0:T(8,128)S(1)} %copy-done.23), kind=kOutput, calls=%fused_computation.26 | convolution fusion | flops 806354944 | bytes 14630912 | tf_op jit(solution)/shard_map/hcik,hcvk->hciv/dot_general | solution.py:118
  451.8 8.4 %all-to-all-start.2 = ((f32[4096,1,128]{2,1,0:T(1,128)}), f32[4096,1,128]{2,1,0:T(1,128)}, u32[]{:S(2)}, u32[]{:S(2)}) async-start(f32[4096,1,128]{2,1,0:T(1,128)} %bitcast.235), calls=%async_computation.2 | async-start | bytes 4194304 | tf_op jit(solution)/shard_map/all_to_all | solution.py:120
  460.2 7.7 %fusion.84 = f32[2048,512]{1,0:T(8,128)S(1)} fusion(bf16[2048,2048]{1,0:T(8,128)(2,1)} %bitcast.73, bf16[1,2048,512]{2,1,0:T(8,128)(2,1)} %param.31), kind=kOutput, calls=%fused_computation.92 | convolution fusion | flops 4294967296 | bytes 14680064 | tf_op jit(solution)/shard_map/dot_general | solution.py:187
  467.9 8.8 %multiply_convert_fusion = bf16[2048,512]{1,0:T(8,128)(2,1)S(1)} fusion(f32[2048,512]{1,0:T(8,128)S(1)} %fusion.84, bf16[2048,2048]{1,0:T(8,128)(2,1)} %bitcast.73, bf16[1,2048,512]{2,1,0:T(8,128)(2,1)S(1)} %copy-done.31), kind=kOutput, calls=%fused_computation.62 | convolution fusion | flops 4301258752 | bytes 16777216 | tf_op jit(solution)/shard_map/dot_general | solution.py:188
  487.9 7.6 %all-to-all-start.4 = ((bf16[128,16,2048]{2,1,0:T(8,128)(2,1)}), bf16[128,16,2048]{2,1,0:T(8,128)(2,1)}, u32[]{:S(2)}, u32[]{:S(2)}) async-start(bf16[128,16,2048]{2,1,0:T(8,128)(2,1)} %bitcast.233), calls=%async_computation.4 | async-start | bytes 16777216 | tf_op jit(solution)/shard_map/all_to_all | solution.py:191
  505.6 99.4 %collective-permute-done = bf16[1,128,1024]{1,2,0:T(8,128)(2,1)} collective-permute-done((bf16[1,128,1024]{1,2,0:T(8,128)(2,1)S(1)}, bf16[1,128,1024]{1,2,0:T(8,128)(2,1)}, u32[]{:S(2)}, u32[]{:S(2)}) %collective-permute-start) | collective-permute-done | bytes 262176 | tf_op jit(solution)/shard_map/ppermute | solution.py:24
  627.1 15.3 %gather_fusion = bf16[1280,2048]{1,0:T(8,128)(2,1)} fusion(bf16[2048,2048]{1,0:T(8,128)(2,1)} %bitcast.78, s32[2048]{0:T(1024)S(1)} %pad_clamp_fusion), kind=kCustom, calls=%fused_computation | custom fusion | bytes 10490880 | tf_op jit(solution)/shard_map/gather | solution.py:194
  642.5 9.6 %reshape.565 = bf16[128,10,2048]{2,1,0:T(8,128)(2,1)} reshape(bf16[1280,2048]{1,0:T(8,128)(2,1)} %gather_fusion) | data formatting | bytes 10485760 | tf_op jit(solution)/shard_map/reshape | solution.py:198
  (169 shorter events, 187.5 us)
Async XLA Ops:
  0.6 476.1 %copy-start = (bf16[1,512,2048]{2,1,0:T(8,128)(2,1)S(1)}, bf16[1,512,2048]{2,1,0:T(8,128)(2,1)}, u32[]{:S(2)}) copy-start(bf16[1,512,2048]{2,1,0:T(8,128)(2,1)} %param.33) | copy-start | bytes 6291460
  2.2 23.3 %all-to-all-start = ((f32[2,32,128]{2,0,1:T(2,128)}), f32[2,32,128]{2,0,1:T(2,128)S(1)}, u32[]{:S(2)}, u32[]{:S(2)}) async-start(f32[2,32,128]{2,0,1:T(2,128)} %copy.114), calls=%async_computation | async-start | bytes 65536 | tf_op jit(solution)/shard_map/all_to_all | solution.py:99
  20.8 12.2 %copy-start.26 = (s32[1,128,10]{1,0,2:T(1,128)S(1)}, s32[1,128,10]{1,0,2:T(1,128)}, u32[]{:S(2)}) copy-start(s32[1,128,10]{1,0,2:T(1,128)} %param.28) | copy-start | bytes 15364
  25.4 9.0 %copy-start.22 = (bf16[1,128,2048]{2,1,0:T(8,128)(2,1)S(1)}, bf16[1,128,2048]{2,1,0:T(8,128)(2,1)}, u32[]{:S(2)}) copy-start(bf16[1,128,2048]{2,1,0:T(8,128)(2,1)} %param.27) | copy-start | bytes 1572868
  25.4 47.5 %all-to-all-start.1 = ((bf16[128,32,384]{2,0,1:T(8,128)(2,1)}), bf16[128,32,384]{2,0,1:T(8,128)(2,1)}, u32[]{:S(2)}, u32[]{:S(2)}) async-start(bf16[128,32,384]{2,0,1:T(8,128)(2,1)} %copy.120), calls=%async_computation.1 | async-start | bytes 6291456 | tf_op jit(solution)/shard_map/all_to_all | solution.py:97
  38.9 9.8 %copy-start.27 = (s32[1,128,10]{1,0,2:T(1,128)S(1)}, s32[1,128,10]{1,0,2:T(1,128)}, u32[]{:S(2)}) copy-start(s32[1,128,10]{1,0,2:T(1,128)} %param.29) | copy-start | bytes 15364
  49.0 19.8 %copy-start.24 = (s32[1280]{0:T(1024)}, s32[1280]{0:T(1024)S(1)}, u32[]{:S(2)}) copy-start(s32[1280]{0:T(1024)S(1)} %fusion.112) | copy-start | bytes 15364
  72.9 378.8 %all-to-all-start.3 = ((bf16[128,16,2048]{2,1,0:T(8,128)(2,1)}), bf16[128,16,2048]{2,1,0:T(8,128)(2,1)}, u32[]{:S(2)}, u32[]{:S(2)}) async-start(bf16[128,16,2048]{2,1,0:T(8,128)(2,1)} %bitcast.230), calls=%async_computation.3 | async-start | bytes 16777216 | tf_op jit(solution)/shard_map/all_to_all | solution.py:179
  137.2 14.1 %copy-start.11 = (f32[1,128,32,256]{3,2,1,0:T(8,128)}, f32[1,128,32,256]{3,2,1,0:T(8,128)S(1)}, u32[]{:S(2)}) copy-start(f32[1,128,32,256]{3,2,1,0:T(8,128)S(1)} %fusion.76) | copy-start | bytes 12582916
  151.3 14.2 %copy-start.8 = (f32[128,128,128]{2,1,0:T(8,128)}, f32[128,128,128]{2,1,0:T(8,128)S(1)}, u32[]{:S(2)}) copy-start(f32[128,128,128]{2,1,0:T(8,128)S(1)} %fusion.92) | copy-start | bytes 25165828
  187.9 7.8 %copy-start.9 = (f32[128,128,128]{2,1,0:T(8,128)S(1)}, f32[128,128,128]{2,1,0:T(8,128)}, u32[]{:S(2)}) copy-start(f32[128,128,128]{2,1,0:T(8,128)} %fusion.54) | copy-start | bytes 25165828
  212.5 16.7 %copy-start.1 = (f32[128,128,128]{2,1,0:T(8,128)S(1)}, f32[128,128,128]{2,1,0:T(8,128)}, u32[]{:S(2)}) copy-start(f32[128,128,128]{2,1,0:T(8,128)} %fusion) | copy-start | bytes 25165828
  229.2 6.4 copy-start.10
  251.8 7.7 %copy-start.2 = (f32[128,128,128]{2,1,0:T(8,128)S(1)}, f32[128,128,128]{2,1,0:T(8,128)}, u32[]{:S(2)}) copy-start(f32[128,128,128]{2,1,0:T(8,128)} %fusion.3) | copy-start | bytes 25165828
  292.9 7.4 %copy-start.3 = (f32[128,128,128]{2,1,0:T(8,128)S(1)}, f32[128,128,128]{2,1,0:T(8,128)}, u32[]{:S(2)}) copy-start(f32[128,128,128]{2,1,0:T(8,128)} %fusion.6) | copy-start | bytes 25165828
  313.9 7.3 %copy-start.13 = (f32[1,120,128,128]{3,2,1,0:T(8,128)S(1)}, f32[1,120,128,128]{3,2,1,0:T(8,128)}, u32[]{:S(2)}) copy-start(f32[1,120,128,128]{3,2,1,0:T(8,128)} %slice.149) | copy-start | bytes 23592964
  332.3 7.1 %copy-start.4 = (f32[128,128,128]{2,1,0:T(8,128)S(1)}, f32[128,128,128]{2,1,0:T(8,128)}, u32[]{:S(2)}) copy-start(f32[128,128,128]{2,1,0:T(8,128)} %fusion.9) | copy-start | bytes 25165828
  371.5 6.4 copy-start.5
  424.7 7.4 %copy-start.23 = (f32[128,32]{1,0:T(8,128)S(1)}, f32[128,32]{1,0:T(8,128)}, u32[]{:S(2)}) copy-start(f32[128,32]{1,0:T(8,128)} %copy.116) | copy-start | bytes 49156
  432.2 15.9 %copy-start.12 = (f32[1,128,32,256]{3,2,1,0:T(8,128)S(1)}, f32[1,128,32,256]{3,2,1,0:T(8,128)}, u32[]{:S(2)}) copy-start(f32[1,128,32,256]{3,2,1,0:T(8,128)} %copy-done.11) | copy-start | bytes 12582916
  432.2 15.9 %copy-start.16 = (f32[128,32,32]{2,1,0:T(8,128)S(1)}, f32[128,32,32]{2,1,0:T(8,128)}, u32[]{:S(2)}) copy-start(f32[128,32,32]{2,1,0:T(8,128)} %copy.127) | copy-start | bytes 1572868
  451.8 36.2 %all-to-all-start.2 = ((f32[4096,1,128]{2,1,0:T(1,128)}), f32[4096,1,128]{2,1,0:T(1,128)}, u32[]{:S(2)}, u32[]{:S(2)}) async-start(f32[4096,1,128]{2,1,0:T(1,128)} %bitcast.235), calls=%async_computation.2 | async-start | bytes 4194304 | tf_op jit(solution)/shard_map/all_to_all | solution.py:120
  460.2 7.7 %copy-start.31 = (bf16[1,2048,512]{2,1,0:T(8,128)(2,1)S(1)}, bf16[1,2048,512]{2,1,0:T(8,128)(2,1)}, u32[]{:S(2)}) copy-start(bf16[1,2048,512]{2,1,0:T(8,128)(2,1)} %param.32) | copy-start | bytes 6291460
  487.9 10.8 %copy-start.25 = (s32[1280]{0:T(1024)S(1)}, s32[1280]{0:T(1024)}, u32[]{:S(2)}) copy-start(s32[1280]{0:T(1024)} %copy-done.24) | copy-start | bytes 15364
  487.9 10.9 %copy-start.28 = (s32[1,128,10]{1,0,2:T(1,128)S(1)}, s32[1,128,10]{1,0,2:T(1,128)}, u32[]{:S(2)}) copy-start(s32[1,128,10]{1,0,2:T(1,128)} %param.29) | copy-start | bytes 15364
  487.9 10.9 %copy-start.29 = (f32[1,128,10]{1,0,2:T(1,128)S(1)}, f32[1,128,10]{1,0,2:T(1,128)}, u32[]{:S(2)}) copy-start(f32[1,128,10]{1,0,2:T(1,128)} %param.30) | copy-start | bytes 15364
  487.9 10.9 %copy-start.30 = (f32[128]{0:T(128)S(1)}, f32[128]{0:T(128)}, u32[]{:S(2)}) copy-start(f32[128]{0:T(128)} %param.23) | copy-start | bytes 1540
  487.9 10.9 %copy-start.20 = (bf16[1,128,4096]{2,1,0:T(8,128)(2,1)S(1)}, bf16[1,128,4096]{2,1,0:T(8,128)(2,1)}, u32[]{:S(2)}) copy-start(bf16[1,128,4096]{2,1,0:T(8,128)(2,1)} %param.26) | copy-start | bytes 3145732
  487.9 139.2 %all-to-all-start.4 = ((bf16[128,16,2048]{2,1,0:T(8,128)(2,1)}), bf16[128,16,2048]{2,1,0:T(8,128)(2,1)}, u32[]{:S(2)}, u32[]{:S(2)}) async-start(bf16[128,16,2048]{2,1,0:T(8,128)(2,1)} %bitcast.233), calls=%async_computation.4 | async-start | bytes 16777216 | tf_op jit(solution)/shard_map/all_to_all | solution.py:191
  496.7 108.3 %collective-permute-start = (bf16[1,128,1024]{1,2,0:T(8,128)(2,1)S(1)}, bf16[1,128,1024]{1,2,0:T(8,128)(2,1)}, u32[]{:S(2)}, u32[]{:S(2)}) collective-permute-start(bf16[1,128,1024]{1,2,0:T(8,128)(2,1)S(1)} %copy.133), channel_id=1, source_target_pairs={{0,1},{1,2},{2,3},{3,4},{4,5},{5,6},{6,7},{7,8},{8,9},{9,10},{10,1... | collective-permute-start | bytes 786440 | tf_op jit(solution)/shard_map/ppermute | solution.py:24
  505.5 101.8 %copy-start.18 = (f32[1,128,4096]{1,2,0:T(8,128)S(1)}, f32[1,128,4096]{1,2,0:T(8,128)}, u32[]{:S(2)}) copy-start(f32[1,128,4096]{1,2,0:T(8,128)} %copy.138) | copy-start | bytes 6291460
  613.4 9.8 %copy-start.21 = (bf16[1,128,4096]{2,1,0:T(8,128)(2,1)S(1)}, bf16[1,128,4096]{2,1,0:T(8,128)(2,1)}, u32[]{:S(2)}) copy-start(bf16[1,128,4096]{2,1,0:T(8,128)(2,1)} %param.20) | copy-start | bytes 3145732
  (6 other events, 26.2 us)
